TPU v7x, 512 devices: a whole 4x4x16 slice. The times are simulated.
512 devices in a mesh: ctx: 64 (over z, y_hi, core), head: 8 (over y_lo, x).
Axes of the slice: x: 4, y: 4 (y_hi: 2, y_lo: 2; y = y_hi * 2 + y_lo), z: 16, core: 2. Of those that a mesh axis runs over, the one named last changes fastest.
Arguments:
- query_states: bfloat16 [32768, 8192], P('ctx', 'head'), may hold values from -5 to 5
- key_states: bfloat16 [32768, 1024], P('ctx', 'head'), may hold values from -5 to 5
- value_states: bfloat16 [32768, 1024], P('ctx', 'head'), may hold values from -6 to 6
- out_grad: bfloat16 [32768, 8192], P('ctx', 'head'), may hold values from -6 to 6
- block_lists: int32 [256, 4], replicated, may hold values from 0 to 255, as said below
Outputs:
- query_grad: bfloat16 [32768, 8192], P(('ctx', 'head'))
- key_grad: bfloat16 [32768, 1024], P(('ctx', 'head'))
- value_grad: bfloat16 [32768, 1024], P(('ctx', 'head'))
Inputs may be any that keep to these rules, and one draw needn't show every extreme that they name: `block_lists`: entry 0 of row b is b. The other entries name distinct blocks below b, each held by the same index of ctx as b or by one of the 8 indices just below it; a row with fewer candidates repeats b in its remaining entries. Taken over the 4 rows of one index of ctx, the listed blocks that another index of ctx holds are at most one distinct block.
All inputs are finite; a program needn't handle non-finite values.
Results may differ from a plain program's by a relative error of at most 0.012.
Values may be sent and summed in bfloat16 or wider, within the bound.
No kernel may reach another device: no remote copies, remote signals or barrier semaphores. Data moves between devices by JAX's collectives and lax.ppermute only.
A program may use at most 64 MiB of HBM per device.

v0:
```python
import functools
import math

import jax
import jax.numpy as jnp
from jax import lax
from jax.experimental import pallas as pl
from jax.experimental.pallas import tpu as pltpu
from jax.sharding import PartitionSpec as P


HEAD_DIM = 128
BLOCK = 128
REACH = 8


def from_behind(x, axis, by):
    devices = lax.axis_size(axis)
    pairs = [(i, i + by) for i in range(devices) if 0 <= i + by < devices]
    return lax.ppermute(x, axis, pairs)


def requests_of(lists_pad, owner, blocks_here):
    rows = lax.dynamic_slice_in_dim(lists_pad, owner + 1, REACH, 0)
    mine = rows // blocks_here == owner
    return jnp.max(jnp.where(mine, rows % blocks_here, -1), axis=1)


def fetch_tree(kv_local, lists_pad, myself):
    blocks_here = kv_local.shape[0]
    kv_prev = from_behind(kv_local, "ctx", 1)
    req_me = jnp.clip(requests_of(lists_pad, myself, blocks_here), 0, blocks_here - 1)
    req_prev = jnp.clip(requests_of(lists_pad, myself - 1, blocks_here), 0, blocks_here - 1)
    out_me = jnp.take(kv_local, req_me, axis=0)
    out_prev = jnp.take(kv_prev, req_prev[jnp.array([0, 2, 4, 6])], axis=0)
    step2 = from_behind(jnp.stack([out_me[1], out_prev[1], out_me[5], out_prev[3]]), "ctx", 2)
    step4 = from_behind(jnp.stack([out_me[3], out_prev[2], step2[2], step2[3]]), "ctx", 4)
    step8 = from_behind(out_me[7], "ctx", 8)
    return jnp.stack([out_prev[0], step2[0], step2[1], step4[0], step4[1], step4[2], step4[3], step8])


def return_tree(first, rest):
    step4 = from_behind(first, "ctx", -4)
    step8 = from_behind(rest[3], "ctx", -8)
    step2 = from_behind(jnp.stack([rest[1], rest[2], step4[2], step4[3]]), "ctx", -2)
    step1 = from_behind(jnp.stack([rest[0], step2[1], step4[1], step2[3]]), "ctx", -1)
    return jnp.stack([step1[0], step2[0], step1[1], step4[0], step1[2], step2[2], step1[3], step8])


def attn_kernel(slot_ref, use_ref, early_ref, q_ref, g_ref, kv_ref, dq_ref, home_ref, first_ref, rest_ref, kv_scr,
                qs_scr, gs_scr,
                acc_ref, *, chosen, group, scaling):
    n = pl.program_id(0)
    homes = home_ref.shape[0]

    @pl.when(n == 0)
    def _():
        acc_ref[...] = jnp.zeros_like(acc_ref)

    keys = chosen * BLOCK
    for e in range(chosen):
        kv_scr[e * BLOCK:(e + 1) * BLOCK, :] = kv_ref[slot_ref[n * chosen + e]]
    key_cat = kv_scr[:, :HEAD_DIM]
    value_cat = kv_scr[:, HEAD_DIM:]
    for h in range(group):
        qs_scr[h * BLOCK:(h + 1) * BLOCK, :] = q_ref[:, h * HEAD_DIM:(h + 1) * HEAD_DIM]
        gs_scr[h * BLOCK:(h + 1) * BLOCK, :] = g_ref[:, h * HEAD_DIM:(h + 1) * HEAD_DIM]
    q_all = qs_scr[...]
    g_all = gs_scr[...]

    col = lax.broadcasted_iota(jnp.int32, (BLOCK, keys), 1)
    row = lax.broadcasted_iota(jnp.int32, (BLOCK, keys), 0)
    ent = col // BLOCK
    tok = col % BLOCK
    use_col = jnp.zeros((BLOCK, keys), jnp.int32)
    early_col = jnp.zeros((BLOCK, keys), jnp.int32)
    for e in range(chosen):
        use_col = jnp.where(ent == e, use_ref[n * chosen + e], use_col)
        early_col = jnp.where(ent == e, early_ref[n * chosen + e], early_col)
    allowed = (use_col != 0) & ((early_col != 0) | (tok <= row))

    nt = (((1,), (1,)), ((), ()))
    tn = (((0,), (0,)), ((), ()))
    rows = group * BLOCK
    scores = lax.dot_general(q_all, key_cat, nt, preferred_element_type=jnp.float32) * scaling
    scores = scores.reshape(group, BLOCK, keys)
    scores = jnp.where(allowed[None], scores, -1e30)
    row_max = jnp.max(scores, axis=2, keepdims=True)
    total = jnp.sum(jnp.exp(scores - row_max), axis=2, keepdims=True)
    log_total = row_max + jnp.log(total)
    prob = jnp.exp(scores - log_total).reshape(rows, keys)
    prob_half = prob.astype(jnp.bfloat16)
    output = jnp.dot(prob_half, value_cat, preferred_element_type=jnp.float32)
    output = output.astype(jnp.bfloat16).astype(jnp.float32)
    row_dot = jnp.sum(g_all.astype(jnp.float32) * output, axis=1, keepdims=True)
    prob_grad = lax.dot_general(g_all, value_cat, nt, preferred_element_type=jnp.float32)
    score_grad = (prob * (prob_grad - row_dot) * scaling).astype(jnp.bfloat16)
    dq_all = jnp.dot(score_grad, key_cat, preferred_element_type=jnp.float32).astype(jnp.bfloat16)
    for h in range(group):
        dq_ref[:, h * HEAD_DIM:(h + 1) * HEAD_DIM] = dq_all[h * BLOCK:(h + 1) * BLOCK, :]
    key_t = lax.dot_general(q_all, score_grad, tn, preferred_element_type=jnp.float32)
    value_t = lax.dot_general(g_all, prob_half, tn, preferred_element_type=jnp.float32)
    key_part = key_t.T
    value_part = value_t.T

    for e in range(chosen):
        s = slot_ref[n * chosen + e]
        part = slice(e * BLOCK, (e + 1) * BLOCK)
        acc_ref[s, :, :HEAD_DIM] += key_part[part, :]
        acc_ref[s, :, HEAD_DIM:] += value_part[part, :]

    @pl.when(n == pl.num_programs(0) - 1)
    def _():
        home_ref[...] = acc_ref[:homes]
        first_ref[...] = acc_ref[homes + 3:homes + 7].astype(jnp.bfloat16)
        rest_ref[0:3] = acc_ref[homes:homes + 3].astype(jnp.bfloat16)
        rest_ref[3] = acc_ref[homes + 7].astype(jnp.bfloat16)


def attention_terms(slots, usable, earlier, query_states, out_grad, kv_stock, chosen):
    tok_rows, q_cols = query_states.shape
    slot_count = kv_stock.shape[0]
    group = q_cols // HEAD_DIM
    blocks_here = tok_rows // BLOCK
    kernel = functools.partial(attn_kernel, chosen=chosen, group=group, scaling=1.0 / math.sqrt(HEAD_DIM))
    grid_spec = pltpu.PrefetchScalarGridSpec(
        num_scalar_prefetch=3,
        grid=(blocks_here,),
        in_specs=[
            pl.BlockSpec((BLOCK, q_cols), lambda n, *_: (n, 0)),
            pl.BlockSpec((BLOCK, q_cols), lambda n, *_: (n, 0)),
            pl.BlockSpec((slot_count, BLOCK, 2 * HEAD_DIM), lambda n, *_: (0, 0, 0)),
        ],
        out_specs=[
            pl.BlockSpec((BLOCK, q_cols), lambda n, *_: (n, 0)),
            pl.BlockSpec((blocks_here, BLOCK, 2 * HEAD_DIM), lambda n, *_: (0, 0, 0)),
            pl.BlockSpec((4, BLOCK, 2 * HEAD_DIM), lambda n, *_: (0, 0, 0)),
            pl.BlockSpec((4, BLOCK, 2 * HEAD_DIM), lambda n, *_: (0, 0, 0)),
        ],
        scratch_shapes=[
            pltpu.VMEM((chosen * BLOCK, 2 * HEAD_DIM), jnp.bfloat16),
            pltpu.VMEM((group * BLOCK, HEAD_DIM), jnp.bfloat16),
            pltpu.VMEM((group * BLOCK, HEAD_DIM), jnp.bfloat16),
            pltpu.VMEM((slot_count, BLOCK, 2 * HEAD_DIM), jnp.float32),
        ],
    )
    return pl.pallas_call(
        kernel,
        grid_spec=grid_spec,
        out_shape=[
            jax.ShapeDtypeStruct((tok_rows, q_cols), jnp.bfloat16),
            jax.ShapeDtypeStruct((blocks_here, BLOCK, 2 * HEAD_DIM), jnp.float32),
            jax.ShapeDtypeStruct((4, BLOCK, 2 * HEAD_DIM), jnp.bfloat16),
            jax.ShapeDtypeStruct((4, BLOCK, 2 * HEAD_DIM), jnp.bfloat16),
        ],
        compiler_params=pltpu.CompilerParams(dimension_semantics=("arbitrary",)),
    )(slots, usable, earlier, query_states, out_grad, kv_stock)


def step(query_states, key_states, value_states, out_grad, block_lists):
    ctx_count = lax.axis_size("ctx")
    head_count = lax.axis_size("head")
    myself = lax.axis_index("ctx")
    tok_rows = query_states.shape[0]
    kv_cols = key_states.shape[1]
    blocks_here = tok_rows // BLOCK
    chosen = block_lists.shape[1]
    lists_by_dev = block_lists.reshape(ctx_count, blocks_here * chosen)
    slot_ids = jnp.arange(blocks_here, dtype=jnp.int32)
    no_rows = jnp.full((REACH, blocks_here * chosen), -blocks_here, jnp.int32)
    lists_pad = jnp.concatenate([lists_by_dev, no_rows], axis=0)
    kv_local = jnp.concatenate([key_states, value_states], axis=1).reshape(blocks_here, BLOCK, 2 * kv_cols)
    kv_stock = jnp.concatenate([kv_local, fetch_tree(kv_local, lists_pad, myself)], axis=0)
    requested = requests_of(lists_pad, myself, blocks_here)

    own_entries = lax.dynamic_slice_in_dim(block_lists, myself * blocks_here, blocks_here, 0)
    block_ids = myself * blocks_here + slot_ids
    order_ids = jnp.arange(chosen, dtype=jnp.int32)
    repeat = (own_entries[:, :, None] == own_entries[:, None, :]) & (
        order_ids[None, None, :] < order_ids[None, :, None]
    )
    usable = jnp.logical_not(jnp.any(repeat, axis=2))
    earlier = own_entries < block_ids[:, None]
    behind = myself - own_entries // blocks_here
    slots = jnp.where(behind == 0, own_entries % blocks_here, blocks_here - 1 + behind)
    slots = jnp.clip(slots, 0, blocks_here + REACH - 1)

    query_local, home, first, rest = attention_terms(
        slots.reshape(-1).astype(jnp.int32),
        usable.reshape(-1).astype(jnp.int32),
        earlier.reshape(-1).astype(jnp.int32),
        query_states,
        out_grad,
        kv_stock,
        chosen,
    )
    query_grad = lax.all_to_all(query_local, "head", split_axis=0, concat_axis=1, tiled=True)
    arrived = return_tree(first, rest).astype(jnp.float32)
    credit = (requested[None, :] == slot_ids[:, None]).astype(jnp.float32)
    totals = home + jnp.sum(credit[:, :, None, None] * arrived[None], axis=1)
    kv_grad = totals.reshape(tok_rows, 2 * kv_cols).astype(jnp.bfloat16)
    kv_all = lax.all_to_all(kv_grad, "head", split_axis=0, concat_axis=1, tiled=True)
    out_rows = tok_rows // head_count
    kv_all = kv_all.reshape(out_rows, head_count, 2, kv_cols)
    key_grad = kv_all[:, :, 0, :].reshape(out_rows, head_count * kv_cols)
    value_grad = kv_all[:, :, 1, :].reshape(out_rows, head_count * kv_cols)
    return (query_grad, key_grad, value_grad)


def solution(mesh):
    in_specs = (P("ctx", "head"), P("ctx", "head"), P("ctx", "head"), P("ctx", "head"), P())
    out_specs = (P(("ctx", "head"), None), P(("ctx", "head"), None), P(("ctx", "head"), None))
    return jax.shard_map(step, mesh=mesh, in_specs=in_specs, out_specs=out_specs, check_vma=False)
```

profile of v0, /device:TPU:96, one launch (start us, length us, event | category | flops | bytes accessed | tf_op | source)
XLA Modules:
  0.0 111.1 jit_solution(12489112430979437668)
XLA Ops:
  0.6 1.0 pad_maximum_fusion
  1.6 1.9 %collective-permute-start = (bf16[4,128,256]{2,1,0:T(8,128)(2,1)S(1)}, bf16[4,128,256]{2,1,0:T(8,128)(2,1)S(1)}, u32[]{:S(2)}, u32[]{:S(2)}) collective-permute-start(bf16[4,128,256]{2,1,0:T(8,128)(2,1)S(1)} %bitcast.38), channel_id=1, source_target_pairs={{0,8},{8,16},{16,24},{24,32},{32,40},{40,48},{48,56},{56,64},{64,7... | collective-permute-start | bytes 786440 | tf_op jit(solution)/shard_map/ppermute | solution.py:20
  3.6 0.8 copy.28
  4.4 0.1 reshape.178
  4.5 0.2 fusion.5
  4.7 0.6 gather_fusion.2
  5.3 0.1 broadcast_select_fusion
  5.5 6.4 %collective-permute-start.3 = (bf16[128,256]{1,0:T(8,128)(2,1)S(1)}, bf16[128,256]{1,0:T(8,128)(2,1)S(1)}, u32[]{:S(2)}, u32[]{:S(2)}) collective-permute-start(bf16[128,256]{1,0:T(8,128)(2,1)S(1)} %get-tuple-element.15), channel_id=1, source_target_pairs={{0,64},{8,72},{16,80},{24,88},{32,96},{40,104},{48,112},{56,120},{... | collective-permute-start | bytes 196616 | tf_op jit(solution)/shard_map/ppermute | solution.py:20
  11.9 0.6 gather_fusion
  12.6 0.1 compare_convert_fusion
  12.7 0.6 gather_fusion.1
  13.3 0.1 broadcast_select_fusion.1
  13.4 5.1 %collective-permute-start.1 = (bf16[4,128,256]{2,1,0:T(8,128)(2,1)S(1)}, bf16[4,128,256]{2,1,0:T(8,128)(2,1)S(1)}, u32[]{:S(2)}, u32[]{:S(2)}) collective-permute-start(bf16[4,128,256]{2,1,0:T(8,128)(2,1)S(1)} %pad_maximum_fusion.1), channel_id=1, source_target_pairs={{0,16},{8,24},{16,32},{24,40},{32,48},{40,56},{48,64},{56,72},{64,... | collective-permute-start | bytes 786440 | tf_op jit(solution)/shard_map/ppermute | solution.py:20
  18.5 0.1 copy.25
  18.7 6.2 %collective-permute-done.1 = bf16[4,128,256]{2,1,0:T(8,128)(2,1)S(1)} collective-permute-done((bf16[4,128,256]{2,1,0:T(8,128)(2,1)S(1)}, bf16[4,128,256]{2,1,0:T(8,128)(2,1)S(1)}, u32[]{:S(2)}, u32[]{:S(2)}) %collective-permute-start.1) | collective-permute-done | bytes 262176 | tf_op jit(solution)/shard_map/ppermute | solution.py:20
  24.9 8.0 %collective-permute-start.2 = (bf16[4,128,256]{2,1,0:T(8,128)(2,1)S(1)}, bf16[4,128,256]{2,1,0:T(8,128)(2,1)S(1)}, u32[]{:S(2)}, u32[]{:S(2)}) collective-permute-start(bf16[4,128,256]{2,1,0:T(8,128)(2,1)S(1)} %pad_maximum_fusion.2), channel_id=1, source_target_pairs={{0,32},{8,40},{16,48},{24,56},{32,64},{40,72},{48,80},{56,88},{64,... | collective-permute-start | bytes 786440 | tf_op jit(solution)/shard_map/ppermute | solution.py:20
  32.9 0.2 and_reduce_fusion
  33.1 0.1 copy.24
  33.2 0.6 reshape.176.slot_ref
  33.8 0.6 reshape.180.use_ref
  34.4 0.1 copy.27
  34.5 0.6 reshape.181.early_ref
  35.1 3.9 %collective-permute-done.2 = bf16[4,128,256]{2,1,0:T(8,128)(2,1)S(1)} collective-permute-done((bf16[4,128,256]{2,1,0:T(8,128)(2,1)S(1)}, bf16[4,128,256]{2,1,0:T(8,128)(2,1)S(1)}, u32[]{:S(2)}, u32[]{:S(2)}) %collective-permute-start.2) | collective-permute-done | bytes 262176 | tf_op jit(solution)/shard_map/ppermute | solution.py:20
  39.1 0.9 copy-done
  40.0 12.8 %shard_map.85 = (bf16[512,1024]{1,0:T(8,128)(2,1)}, f32[4,128,256]{2,1,0:T(8,128)}, bf16[4,128,256]{2,1,0:T(8,128)(2,1)}, bf16[4,128,256]{2,1,0:T(8,128)(2,1)}) custom-call(s32[16]{0:T(128)} %reshape.176.slot_ref, s32[16]{0:T(128)} %reshape.180.use_ref, s32[16]{0:T(128)} %reshape.181.early_ref, bf16[512,1024]{1,0:T(8,128)(2,1)} %q_ref.1, ...), custom_call_target="tpu_custom_call" | custom-call | tf_op jit(solution)/shard_map/pallas_call | solution.py:147
  52.8 2.1 %collective-permute-start.4 = (bf16[4,128,256]{2,1,0:T(8,128)(2,1)}, bf16[4,128,256]{2,1,0:T(8,128)(2,1)S(1)}, u32[]{:S(2)}, u32[]{:S(2)}) collective-permute-start(bf16[4,128,256]{2,1,0:T(8,128)(2,1)} %get-tuple-element.10), channel_id=1, source_target_pairs={{32,0},{40,8},{48,16},{56,24},{64,32},{72,40},{80,48},{88,56},{96,... | collective-permute-start | bytes 786440 | tf_op jit(solution)/shard_map/ppermute | solution.py:20
  54.9 0.9 slice.102
  55.8 9.0 %collective-permute-done.4 = bf16[4,128,256]{2,1,0:T(8,128)(2,1)S(1)} collective-permute-done((bf16[4,128,256]{2,1,0:T(8,128)(2,1)}, bf16[4,128,256]{2,1,0:T(8,128)(2,1)S(1)}, u32[]{:S(2)}, u32[]{:S(2)}) %collective-permute-start.4) | collective-permute-done | bytes 262176 | tf_op jit(solution)/shard_map/ppermute | solution.py:20
  64.8 1.9 %collective-permute-start.5 = (bf16[4,128,256]{2,1,0:T(8,128)(2,1)S(1)}, bf16[4,128,256]{2,1,0:T(8,128)(2,1)S(1)}, u32[]{:S(2)}, u32[]{:S(2)}) collective-permute-start(bf16[4,128,256]{2,1,0:T(8,128)(2,1)S(1)} %pad_maximum_fusion.3), channel_id=1, source_target_pairs={{16,0},{24,8},{32,16},{40,24},{48,32},{56,40},{64,48},{72,56},{80,... | collective-permute-start | bytes 786440 | tf_op jit(solution)/shard_map/ppermute | solution.py:20
  66.8 8.6 %collective-permute-done.5 = bf16[4,128,256]{2,1,0:T(8,128)(2,1)S(1)} collective-permute-done((bf16[4,128,256]{2,1,0:T(8,128)(2,1)S(1)}, bf16[4,128,256]{2,1,0:T(8,128)(2,1)S(1)}, u32[]{:S(2)}, u32[]{:S(2)}) %collective-permute-start.5) | collective-permute-done | bytes 262176 | tf_op jit(solution)/shard_map/ppermute | solution.py:20
  75.4 1.9 %collective-permute-start.6 = (bf16[4,128,256]{2,1,0:T(8,128)(2,1)S(1)}, bf16[4,128,256]{2,1,0:T(8,128)(2,1)S(1)}, u32[]{:S(2)}, u32[]{:S(2)}) collective-permute-start(bf16[4,128,256]{2,1,0:T(8,128)(2,1)S(1)} %pad_maximum_fusion.4), channel_id=1, source_target_pairs={{8,0},{16,8},{24,16},{32,24},{40,32},{48,40},{56,48},{64,56},{72,6... | collective-permute-start | bytes 786440 | tf_op jit(solution)/shard_map/ppermute | solution.py:20
  77.4 4.3 %all-to-all-start = ((bf16[8,64,1024]{2,1,0:T(8,128)(2,1)}), bf16[8,64,1024]{2,1,0:T(8,128)(2,1)S(1)}, u32[]{:S(2)}, u32[]{:S(2)}) async-start(bf16[8,64,1024]{2,1,0:T(8,128)(2,1)} %bitcast.7), calls=%async_computation | async-start | bytes 2097152 | tf_op jit(solution)/shard_map/all_to_all | solution.py:197
  81.7 1.9 %collective-permute-start.7 = (bf16[128,256]{1,0:T(8,128)(2,1)S(1)}, bf16[128,256]{1,0:T(8,128)(2,1)S(1)}, u32[]{:S(2)}, u32[]{:S(2)}) collective-permute-start(bf16[128,256]{1,0:T(8,128)(2,1)S(1)} %get-tuple-element.21), channel_id=1, source_target_pairs={{64,0},{72,8},{80,16},{88,24},{96,32},{104,40},{112,48},{120,56},{... | collective-permute-start | bytes 196616 | tf_op jit(solution)/shard_map/ppermute | solution.py:20
  83.7 7.3 %collective-permute-done.7 = bf16[128,256]{1,0:T(8,128)(2,1)S(1)} collective-permute-done((bf16[128,256]{1,0:T(8,128)(2,1)S(1)}, bf16[128,256]{1,0:T(8,128)(2,1)S(1)}, u32[]{:S(2)}, u32[]{:S(2)}) %collective-permute-start.7) | collective-permute-done | bytes 65568 | tf_op jit(solution)/shard_map/ppermute | solution.py:20
  91.0 0.1 convert_element_type.36
  91.1 0.4 multiply_reduce_fusion
  91.5 0.7 copy-done.1
  92.1 0.8 add_convert_fusion
  92.9 5.2 %all-to-all-done = bf16[8,64,1024]{2,1,0:T(8,128)(2,1)S(1)} async-done(((bf16[8,64,1024]{2,1,0:T(8,128)(2,1)}), bf16[8,64,1024]{2,1,0:T(8,128)(2,1)S(1)}, u32[]{:S(2)}, u32[]{:S(2)}) %all-to-all-start) | async-done | bytes 1048608 | tf_op jit(solution)/shard_map/all_to_all | solution.py:197
  98.1 3.4 %all-to-all-start.1 = ((bf16[8,64,256]{2,1,0:T(8,128)(2,1)}), bf16[8,64,256]{2,1,0:T(8,128)(2,1)S(1)}, u32[]{:S(2)}, u32[]{:S(2)}) async-start(bf16[8,64,256]{2,1,0:T(8,128)(2,1)} %bitcast.11), calls=%async_computation.1 | async-start | bytes 524288 | tf_op jit(solution)/shard_map/all_to_all | solution.py:202
  101.5 1.1 copy.34
  102.5 6.3 %all-to-all-done.1 = bf16[8,64,256]{2,1,0:T(8,128)(2,1)S(1)} async-done(((bf16[8,64,256]{2,1,0:T(8,128)(2,1)}), bf16[8,64,256]{2,1,0:T(8,128)(2,1)S(1)}, u32[]{:S(2)}, u32[]{:S(2)}) %all-to-all-start.1) | async-done | bytes 262176 | tf_op jit(solution)/shard_map/all_to_all | solution.py:202
  108.9 0.1 reshape.179
  108.9 0.5 fusion.17
  109.4 0.2 copy.32
  109.6 0.7 copy.40
  110.2 0.2 copy.33
  110.4 0.7 copy.39
  (44 shorter events, 0.4 us)
Async XLA Ops:
  1.6 11.1 %collective-permute-start = (bf16[4,128,256]{2,1,0:T(8,128)(2,1)S(1)}, bf16[4,128,256]{2,1,0:T(8,128)(2,1)S(1)}, u32[]{:S(2)}, u32[]{:S(2)}) collective-permute-start(bf16[4,128,256]{2,1,0:T(8,128)(2,1)S(1)} %bitcast.38), channel_id=1, source_target_pairs={{0,8},{8,16},{16,24},{24,32},{32,40},{40,48},{48,56},{56,64},{64,7... | collective-permute-start | bytes 786440 | tf_op jit(solution)/shard_map/ppermute | solution.py:20
  5.4 7.2 %copy-start.3 = (s32[256,4]{0,1:T(4,128)S(1)}, s32[256,4]{0,1:T(4,128)}, u32[]{:S(2)}) copy-start(s32[256,4]{0,1:T(4,128)} %param.10) | copy-start | bytes 12292
  5.5 33.6 %collective-permute-start.3 = (bf16[128,256]{1,0:T(8,128)(2,1)S(1)}, bf16[128,256]{1,0:T(8,128)(2,1)S(1)}, u32[]{:S(2)}, u32[]{:S(2)}) collective-permute-start(bf16[128,256]{1,0:T(8,128)(2,1)S(1)} %get-tuple-element.15), channel_id=1, source_target_pairs={{0,64},{8,72},{16,80},{24,88},{32,96},{40,104},{48,112},{56,120},{... | collective-permute-start | bytes 196616 | tf_op jit(solution)/shard_map/ppermute | solution.py:20
  13.4 11.4 %collective-permute-start.1 = (bf16[4,128,256]{2,1,0:T(8,128)(2,1)S(1)}, bf16[4,128,256]{2,1,0:T(8,128)(2,1)S(1)}, u32[]{:S(2)}, u32[]{:S(2)}) collective-permute-start(bf16[4,128,256]{2,1,0:T(8,128)(2,1)S(1)} %pad_maximum_fusion.1), channel_id=1, source_target_pairs={{0,16},{8,24},{16,32},{24,40},{32,48},{40,56},{48,64},{56,72},{64,... | collective-permute-start | bytes 786440 | tf_op jit(solution)/shard_map/ppermute | solution.py:20
  24.9 14.1 %collective-permute-start.2 = (bf16[4,128,256]{2,1,0:T(8,128)(2,1)S(1)}, bf16[4,128,256]{2,1,0:T(8,128)(2,1)S(1)}, u32[]{:S(2)}, u32[]{:S(2)}) collective-permute-start(bf16[4,128,256]{2,1,0:T(8,128)(2,1)S(1)} %pad_maximum_fusion.2), channel_id=1, source_target_pairs={{0,32},{8,40},{16,48},{24,56},{32,64},{40,72},{48,80},{56,88},{64,... | collective-permute-start | bytes 786440 | tf_op jit(solution)/shard_map/ppermute | solution.py:20
  39.0 0.9 copy-start
  52.8 13.9 %copy-start.2 = (bf16[4,128,256]{2,1,0:T(8,128)(2,1)S(1)}, bf16[4,128,256]{2,1,0:T(8,128)(2,1)}, u32[]{:S(2)}) copy-start(bf16[4,128,256]{2,1,0:T(8,128)(2,1)} %get-tuple-element.9) | copy-start | bytes 786436
  52.8 12.0 %collective-permute-start.4 = (bf16[4,128,256]{2,1,0:T(8,128)(2,1)}, bf16[4,128,256]{2,1,0:T(8,128)(2,1)S(1)}, u32[]{:S(2)}, u32[]{:S(2)}) collective-permute-start(bf16[4,128,256]{2,1,0:T(8,128)(2,1)} %get-tuple-element.10), channel_id=1, source_target_pairs={{32,0},{40,8},{48,16},{56,24},{64,32},{72,40},{80,48},{88,56},{96,... | collective-permute-start | bytes 786440 | tf_op jit(solution)/shard_map/ppermute | solution.py:20
  64.8 10.6 %collective-permute-start.5 = (bf16[4,128,256]{2,1,0:T(8,128)(2,1)S(1)}, bf16[4,128,256]{2,1,0:T(8,128)(2,1)S(1)}, u32[]{:S(2)}, u32[]{:S(2)}) collective-permute-start(bf16[4,128,256]{2,1,0:T(8,128)(2,1)S(1)} %pad_maximum_fusion.3), channel_id=1, source_target_pairs={{16,0},{24,8},{32,16},{40,24},{48,32},{56,40},{64,48},{72,56},{80,... | collective-permute-start | bytes 786440 | tf_op jit(solution)/shard_map/ppermute | solution.py:20
  75.4 8.2 %collective-permute-start.6 = (bf16[4,128,256]{2,1,0:T(8,128)(2,1)S(1)}, bf16[4,128,256]{2,1,0:T(8,128)(2,1)S(1)}, u32[]{:S(2)}, u32[]{:S(2)}) collective-permute-start(bf16[4,128,256]{2,1,0:T(8,128)(2,1)S(1)} %pad_maximum_fusion.4), channel_id=1, source_target_pairs={{8,0},{16,8},{24,16},{32,24},{40,32},{48,40},{56,48},{64,56},{72,6... | collective-permute-start | bytes 786440 | tf_op jit(solution)/shard_map/ppermute | solution.py:20
  77.4 20.7 %all-to-all-start = ((bf16[8,64,1024]{2,1,0:T(8,128)(2,1)}), bf16[8,64,1024]{2,1,0:T(8,128)(2,1)S(1)}, u32[]{:S(2)}, u32[]{:S(2)}) async-start(bf16[8,64,1024]{2,1,0:T(8,128)(2,1)} %bitcast.7), calls=%async_computation | async-start | bytes 2097152 | tf_op jit(solution)/shard_map/all_to_all | solution.py:197
  81.7 9.3 %collective-permute-start.7 = (bf16[128,256]{1,0:T(8,128)(2,1)S(1)}, bf16[128,256]{1,0:T(8,128)(2,1)S(1)}, u32[]{:S(2)}, u32[]{:S(2)}) collective-permute-start(bf16[128,256]{1,0:T(8,128)(2,1)S(1)} %get-tuple-element.21), channel_id=1, source_target_pairs={{64,0},{72,8},{80,16},{88,24},{96,32},{104,40},{112,48},{120,56},{... | collective-permute-start | bytes 196616 | tf_op jit(solution)/shard_map/ppermute | solution.py:20
  91.1 1.0 copy-start.1
  98.1 10.8 %all-to-all-start.1 = ((bf16[8,64,256]{2,1,0:T(8,128)(2,1)}), bf16[8,64,256]{2,1,0:T(8,128)(2,1)S(1)}, u32[]{:S(2)}, u32[]{:S(2)}) async-start(bf16[8,64,256]{2,1,0:T(8,128)(2,1)} %bitcast.11), calls=%async_computation.1 | async-start | bytes 524288 | tf_op jit(solution)/shard_map/all_to_all | solution.py:202
where the time goes:
time: 112 us; the launch traced here: 111 us
  waiting for transfers between devices  46.5 us (42%)
  starting transfers between devices  36.9 us (33%)
  Pallas kernels  12.8 us (11%)
  local copies, waits for them, and re-layouts  10.7 us (10%)
  other arithmetic  3.1 us (3%)
    ppermute x8, waiting for transfers between devices, from_behind(): return lax.ppermute(x, axis, pairs)  35 us
    ppermute x8, starting transfers between devices, from_behind(): return lax.ppermute(x, axis, pairs)  29.2 us
    pallas_call x1, Pallas kernels, attention_terms(): pl.pallas_call(kernel, grid_spec=grid_spec, out_shape=[jax.ShapeDtypeStru...  12.8 us
    all_to_all x1, waiting for transfers between devices, step(): lax.all_to_all(kv_grad, 'head', split_axis=0, concat_axis=1, tiled=True)  6.31 us
    all_to_all x1, waiting for transfers between devices, step(): lax.all_to_all(query_local, 'head', split_axis=0, concat_axis=1, tiled=True)  5.16 us
    all_to_all x1, starting transfers between devices, step(): lax.all_to_all(query_local, 'head', split_axis=0, concat_axis=1, tiled=True)  4.3 us
    unnamed x22, local copies, waits for them, and re-layouts  4.15 us
    all_to_all x1, starting transfers between devices, step(): lax.all_to_all(kv_grad, 'head', split_axis=0, concat_axis=1, tiled=True)  3.41 us
  transfers between devices with their start and end apart: 10, of which 7 were waited for; matrix products, arithmetic and copies ran while one was open for 8% of the time, Pallas kernels for 0%

commit v1 on v0

--- a/solution.py
+++ b/solution.py
@@ -47,7 +47,7 @@
     return jnp.stack([step1[0], step2[0], step1[1], step4[0], step1[2], step2[2], step1[3], step8])
 
 
-def attn_kernel(slot_ref, use_ref, early_ref, q_ref, g_ref, kv_ref, dq_ref, home_ref, first_ref, rest_ref, kv_scr,
+def attn_kernel(slot_ref, use_ref, early_ref, q_ref, g_ref, near_ref, far_ref, dq_ref, home_ref, first_ref, rest_ref, kv_scr,
                 qs_scr, gs_scr,
                 acc_ref, *, chosen, group, scaling):
     n = pl.program_id(0)
@@ -58,8 +58,18 @@
         acc_ref[...] = jnp.zeros_like(acc_ref)
 
     keys = chosen * BLOCK
+    near = near_ref.shape[0]
     for e in range(chosen):
-        kv_scr[e * BLOCK:(e + 1) * BLOCK, :] = kv_ref[slot_ref[n * chosen + e]]
+        slot = slot_ref[n * chosen + e]
+        rows_e = slice(e * BLOCK, (e + 1) * BLOCK)
+
+        @pl.when(slot < near)
+        def _():
+            kv_scr[rows_e, :] = near_ref[jnp.minimum(slot, near - 1)]
+
+        @pl.when(slot >= near)
+        def _():
+            kv_scr[rows_e, :] = far_ref[jnp.maximum(slot - near, 0)]
     key_cat = kv_scr[:, :HEAD_DIM]
     value_cat = kv_scr[:, HEAD_DIM:]
     for h in range(group):
@@ -68,16 +78,16 @@
     q_all = qs_scr[...]
     g_all = gs_scr[...]
 
-    col = lax.broadcasted_iota(jnp.int32, (BLOCK, keys), 1)
-    row = lax.broadcasted_iota(jnp.int32, (BLOCK, keys), 0)
+    col = lax.broadcasted_iota(jnp.int32, (1, keys), 1)
     ent = col // BLOCK
-    tok = col % BLOCK
-    use_col = jnp.zeros((BLOCK, keys), jnp.int32)
-    early_col = jnp.zeros((BLOCK, keys), jnp.int32)
+    use_col = jnp.zeros((1, keys), jnp.int32)
+    early_col = jnp.zeros((1, keys), jnp.int32)
     for e in range(chosen):
         use_col = jnp.where(ent == e, use_ref[n * chosen + e], use_col)
         early_col = jnp.where(ent == e, early_ref[n * chosen + e], early_col)
-    allowed = (use_col != 0) & ((early_col != 0) | (tok <= row))
+    first_row = jnp.where(use_col != 0, jnp.where(early_col != 0, 0, col % BLOCK), BLOCK)
+    row = lax.broadcasted_iota(jnp.int32, (BLOCK, keys), 0)
+    allowed = row >= first_row
 
     nt = (((1,), (1,)), ((), ()))
     tn = (((0,), (0,)), ((), ()))
@@ -117,9 +127,9 @@
         rest_ref[3] = acc_ref[homes + 7].astype(jnp.bfloat16)
 
 
-def attention_terms(slots, usable, earlier, query_states, out_grad, kv_stock, chosen):
+def attention_terms(slots, usable, earlier, query_states, out_grad, kv_near, kv_far, chosen):
     tok_rows, q_cols = query_states.shape
-    slot_count = kv_stock.shape[0]
+    slot_count = kv_near.shape[0] + kv_far.shape[0]
     group = q_cols // HEAD_DIM
     blocks_here = tok_rows // BLOCK
     kernel = functools.partial(attn_kernel, chosen=chosen, group=group, scaling=1.0 / math.sqrt(HEAD_DIM))
@@ -129,7 +139,8 @@
         in_specs=[
             pl.BlockSpec((BLOCK, q_cols), lambda n, *_: (n, 0)),
             pl.BlockSpec((BLOCK, q_cols), lambda n, *_: (n, 0)),
-            pl.BlockSpec((slot_count, BLOCK, 2 * HEAD_DIM), lambda n, *_: (0, 0, 0)),
+            pl.BlockSpec(kv_near.shape, lambda n, *_: (0, 0, 0)),
+            pl.BlockSpec(kv_far.shape, lambda n, *_: (0, 0, 0)),
         ],
         out_specs=[
             pl.BlockSpec((BLOCK, q_cols), lambda n, *_: (n, 0)),
@@ -154,7 +165,7 @@
             jax.ShapeDtypeStruct((4, BLOCK, 2 * HEAD_DIM), jnp.bfloat16),
         ],
         compiler_params=pltpu.CompilerParams(dimension_semantics=("arbitrary",)),
-    )(slots, usable, earlier, query_states, out_grad, kv_stock)
+    )(slots, usable, earlier, query_states, out_grad, kv_near, kv_far)
 
 
 def step(query_states, key_states, value_states, out_grad, block_lists):
@@ -170,7 +181,7 @@
     no_rows = jnp.full((REACH, blocks_here * chosen), -blocks_here, jnp.int32)
     lists_pad = jnp.concatenate([lists_by_dev, no_rows], axis=0)
     kv_local = jnp.concatenate([key_states, value_states], axis=1).reshape(blocks_here, BLOCK, 2 * kv_cols)
-    kv_stock = jnp.concatenate([kv_local, fetch_tree(kv_local, lists_pad, myself)], axis=0)
+    kv_far = fetch_tree(kv_local, lists_pad, myself)
     requested = requests_of(lists_pad, myself, blocks_here)
 
     own_entries = lax.dynamic_slice_in_dim(block_lists, myself * blocks_here, blocks_here, 0)
@@ -191,7 +202,8 @@
         earlier.reshape(-1).astype(jnp.int32),
         query_states,
         out_grad,
-        kv_stock,
+        kv_local,
+        kv_far,
         chosen,
     )
     query_grad = lax.all_to_all(query_local, "head", split_axis=0, concat_axis=1, tiled=True)

time: 112 us -> 112 us (level)
    unnamed x22 -> x20, local copies, waits for them, and re-layouts: 4.15 us -> 3.22 us
where the time goes in v1:
time: 112 us; the launch traced here: 111 us
  waiting for transfers between devices  46.4 us (41%)
  starting transfers between devices  36.9 us (33%)
  Pallas kernels  12.8 us (11%)
  local copies, waits for them, and re-layouts  9.76 us (9%)
  other arithmetic  3.96 us (4%)
    ppermute x8, waiting for transfers between devices, from_behind(): return lax.ppermute(x, axis, pairs)  34.9 us
    ppermute x8, starting transfers between devices, from_behind(): return lax.ppermute(x, axis, pairs)  29.2 us
    pallas_call x1, Pallas kernels, attention_terms(): pl.pallas_call(kernel, grid_spec=grid_spec, out_shape=[jax.ShapeDtypeStru...  12.8 us
    all_to_all x1, waiting for transfers between devices, step(): lax.all_to_all(kv_grad, 'head', split_axis=0, concat_axis=1, tiled=True)  6.31 us
    all_to_all x1, waiting for transfers between devices, step(): lax.all_to_all(query_local, 'head', split_axis=0, concat_axis=1, tiled=True)  5.2 us
    all_to_all x1, starting transfers between devices, step(): lax.all_to_all(query_local, 'head', split_axis=0, concat_axis=1, tiled=True)  4.31 us
    all_to_all x1, starting transfers between devices, step(): lax.all_to_all(kv_grad, 'head', split_axis=0, concat_axis=1, tiled=True)  3.41 us
    unnamed x20, local copies, waits for them, and re-layouts  3.22 us
  transfers between devices with their start and end apart: 10, of which 7 were waited for; matrix products, arithmetic and copies ran while one was open for 8% of the time, Pallas kernels for 0%

profile of v1, /device:TPU:96, one launch (start us, length us, event | category | flops | bytes accessed | tf_op | source)
XLA Modules:
  0.0 111.0 jit_solution(13054083130682262854)
XLA Ops:
  0.6 1.0 pad_maximum_fusion.1
  1.6 1.9 %collective-permute-start = (bf16[4,128,256]{2,1,0:T(8,128)(2,1)S(1)}, bf16[4,128,256]{2,1,0:T(8,128)(2,1)S(1)}, u32[]{:S(2)}, u32[]{:S(2)}) collective-permute-start(bf16[4,128,256]{2,1,0:T(8,128)(2,1)S(1)} %bitcast.37), channel_id=1, source_target_pairs={{0,8},{8,16},{16,24},{24,32},{32,40},{40,48},{48,56},{56,64},{64,7... | collective-permute-start | bytes 786440 | tf_op jit(solution)/shard_map/ppermute | solution.py:20
  3.6 0.8 copy.28
  4.4 0.1 reshape.178
  4.5 0.2 fusion.2
  4.7 0.6 gather_fusion.2
  5.3 0.1 broadcast_select_fusion
  5.5 6.4 %collective-permute-start.3 = (bf16[128,256]{1,0:T(8,128)(2,1)S(1)}, bf16[128,256]{1,0:T(8,128)(2,1)S(1)}, u32[]{:S(2)}, u32[]{:S(2)}) collective-permute-start(bf16[128,256]{1,0:T(8,128)(2,1)S(1)} %get-tuple-element.16), channel_id=1, source_target_pairs={{0,64},{8,72},{16,80},{24,88},{32,96},{40,104},{48,112},{56,120},{... | collective-permute-start | bytes 196616 | tf_op jit(solution)/shard_map/ppermute | solution.py:20
  11.9 0.6 gather_fusion
  12.6 0.1 compare_convert_fusion
  12.7 0.6 gather_fusion.1
  13.2 0.1 broadcast_select_fusion.1
  13.4 5.1 %collective-permute-start.1 = (bf16[4,128,256]{2,1,0:T(8,128)(2,1)S(1)}, bf16[4,128,256]{2,1,0:T(8,128)(2,1)S(1)}, u32[]{:S(2)}, u32[]{:S(2)}) collective-permute-start(bf16[4,128,256]{2,1,0:T(8,128)(2,1)S(1)} %pad_maximum_fusion.2), channel_id=1, source_target_pairs={{0,16},{8,24},{16,32},{24,40},{32,48},{40,56},{48,64},{56,72},{64,... | collective-permute-start | bytes 786440 | tf_op jit(solution)/shard_map/ppermute | solution.py:20
  18.5 0.1 copy.25
  18.7 6.2 %collective-permute-done.1 = bf16[4,128,256]{2,1,0:T(8,128)(2,1)S(1)} collective-permute-done((bf16[4,128,256]{2,1,0:T(8,128)(2,1)S(1)}, bf16[4,128,256]{2,1,0:T(8,128)(2,1)S(1)}, u32[]{:S(2)}, u32[]{:S(2)}) %collective-permute-start.1) | collective-permute-done | bytes 262176 | tf_op jit(solution)/shard_map/ppermute | solution.py:20
  24.9 8.0 %collective-permute-start.2 = (bf16[4,128,256]{2,1,0:T(8,128)(2,1)S(1)}, bf16[4,128,256]{2,1,0:T(8,128)(2,1)S(1)}, u32[]{:S(2)}, u32[]{:S(2)}) collective-permute-start(bf16[4,128,256]{2,1,0:T(8,128)(2,1)S(1)} %pad_maximum_fusion.3), channel_id=1, source_target_pairs={{0,32},{8,40},{16,48},{24,56},{32,64},{40,72},{48,80},{56,88},{64,... | collective-permute-start | bytes 786440 | tf_op jit(solution)/shard_map/ppermute | solution.py:20
  32.9 0.2 and_reduce_fusion
  33.1 0.1 copy.24
  33.2 0.6 reshape.176.slot_ref
  33.8 0.6 reshape.180.use_ref
  34.4 0.1 copy.27
  34.5 0.6 reshape.181.early_ref
  35.1 3.9 %collective-permute-done.2 = bf16[4,128,256]{2,1,0:T(8,128)(2,1)S(1)} collective-permute-done((bf16[4,128,256]{2,1,0:T(8,128)(2,1)S(1)}, bf16[4,128,256]{2,1,0:T(8,128)(2,1)S(1)}, u32[]{:S(2)}, u32[]{:S(2)}) %collective-permute-start.2) | collective-permute-done | bytes 262176 | tf_op jit(solution)/shard_map/ppermute | solution.py:20
  39.0 0.9 pad_maximum_fusion.far_ref
  39.9 12.8 %shard_map.85 = (bf16[512,1024]{1,0:T(8,128)(2,1)}, f32[4,128,256]{2,1,0:T(8,128)}, bf16[4,128,256]{2,1,0:T(8,128)(2,1)}, bf16[4,128,256]{2,1,0:T(8,128)(2,1)}) custom-call(s32[16]{0:T(128)} %reshape.176.slot_ref, s32[16]{0:T(128)} %reshape.180.use_ref, s32[16]{0:T(128)} %reshape.181.early_ref, bf16[512,1024]{1,0:T(8,128)(2,1)} %q_ref.1, ...), custom_call_target="tpu_custom_call" | custom-call | tf_op jit(solution)/shard_map/pallas_call | solution.py:158
  52.7 2.1 %collective-permute-start.4 = (bf16[4,128,256]{2,1,0:T(8,128)(2,1)}, bf16[4,128,256]{2,1,0:T(8,128)(2,1)S(1)}, u32[]{:S(2)}, u32[]{:S(2)}) collective-permute-start(bf16[4,128,256]{2,1,0:T(8,128)(2,1)} %get-tuple-element.10), channel_id=1, source_target_pairs={{32,0},{40,8},{48,16},{56,24},{64,32},{72,40},{80,48},{88,56},{96,... | collective-permute-start | bytes 786440 | tf_op jit(solution)/shard_map/ppermute | solution.py:20
  54.8 0.9 slice.102
  55.7 9.0 %collective-permute-done.4 = bf16[4,128,256]{2,1,0:T(8,128)(2,1)S(1)} collective-permute-done((bf16[4,128,256]{2,1,0:T(8,128)(2,1)}, bf16[4,128,256]{2,1,0:T(8,128)(2,1)S(1)}, u32[]{:S(2)}, u32[]{:S(2)}) %collective-permute-start.4) | collective-permute-done | bytes 262176 | tf_op jit(solution)/shard_map/ppermute | solution.py:20
  64.7 1.9 %collective-permute-start.5 = (bf16[4,128,256]{2,1,0:T(8,128)(2,1)S(1)}, bf16[4,128,256]{2,1,0:T(8,128)(2,1)S(1)}, u32[]{:S(2)}, u32[]{:S(2)}) collective-permute-start(bf16[4,128,256]{2,1,0:T(8,128)(2,1)S(1)} %pad_maximum_fusion.4), channel_id=1, source_target_pairs={{16,0},{24,8},{32,16},{40,24},{48,32},{56,40},{64,48},{72,56},{80,... | collective-permute-start | bytes 786440 | tf_op jit(solution)/shard_map/ppermute | solution.py:20
  66.7 8.6 %collective-permute-done.5 = bf16[4,128,256]{2,1,0:T(8,128)(2,1)S(1)} collective-permute-done((bf16[4,128,256]{2,1,0:T(8,128)(2,1)S(1)}, bf16[4,128,256]{2,1,0:T(8,128)(2,1)S(1)}, u32[]{:S(2)}, u32[]{:S(2)}) %collective-permute-start.5) | collective-permute-done | bytes 262176 | tf_op jit(solution)/shard_map/ppermute | solution.py:20
  75.3 1.9 %collective-permute-start.6 = (bf16[4,128,256]{2,1,0:T(8,128)(2,1)S(1)}, bf16[4,128,256]{2,1,0:T(8,128)(2,1)S(1)}, u32[]{:S(2)}, u32[]{:S(2)}) collective-permute-start(bf16[4,128,256]{2,1,0:T(8,128)(2,1)S(1)} %pad_maximum_fusion.5), channel_id=1, source_target_pairs={{8,0},{16,8},{24,16},{32,24},{40,32},{48,40},{56,48},{64,56},{72,6... | collective-permute-start | bytes 786440 | tf_op jit(solution)/shard_map/ppermute | solution.py:20
  77.3 4.3 %all-to-all-start = ((bf16[8,64,1024]{2,1,0:T(8,128)(2,1)}), bf16[8,64,1024]{2,1,0:T(8,128)(2,1)S(1)}, u32[]{:S(2)}, u32[]{:S(2)}) async-start(bf16[8,64,1024]{2,1,0:T(8,128)(2,1)} %bitcast.7), calls=%async_computation | async-start | bytes 2097152 | tf_op jit(solution)/shard_map/all_to_all | solution.py:209
  81.6 1.9 %collective-permute-start.7 = (bf16[128,256]{1,0:T(8,128)(2,1)S(1)}, bf16[128,256]{1,0:T(8,128)(2,1)S(1)}, u32[]{:S(2)}, u32[]{:S(2)}) collective-permute-start(bf16[128,256]{1,0:T(8,128)(2,1)S(1)} %get-tuple-element.21), channel_id=1, source_target_pairs={{64,0},{72,8},{80,16},{88,24},{96,32},{104,40},{112,48},{120,56},{... | collective-permute-start | bytes 196616 | tf_op jit(solution)/shard_map/ppermute | solution.py:20
  83.6 7.2 %collective-permute-done.7 = bf16[128,256]{1,0:T(8,128)(2,1)S(1)} collective-permute-done((bf16[128,256]{1,0:T(8,128)(2,1)S(1)}, bf16[128,256]{1,0:T(8,128)(2,1)S(1)}, u32[]{:S(2)}, u32[]{:S(2)}) %collective-permute-start.7) | collective-permute-done | bytes 65568 | tf_op jit(solution)/shard_map/ppermute | solution.py:20
  90.8 0.1 convert_element_type.36
  90.9 0.4 multiply_reduce_fusion
  91.3 0.7 copy-done.1
  92.0 0.8 add_convert_fusion
  92.7 5.2 %all-to-all-done = bf16[8,64,1024]{2,1,0:T(8,128)(2,1)S(1)} async-done(((bf16[8,64,1024]{2,1,0:T(8,128)(2,1)}), bf16[8,64,1024]{2,1,0:T(8,128)(2,1)S(1)}, u32[]{:S(2)}, u32[]{:S(2)}) %all-to-all-start) | async-done | bytes 1048608 | tf_op jit(solution)/shard_map/all_to_all | solution.py:209
  97.9 3.4 %all-to-all-start.1 = ((bf16[8,64,256]{2,1,0:T(8,128)(2,1)}), bf16[8,64,256]{2,1,0:T(8,128)(2,1)S(1)}, u32[]{:S(2)}, u32[]{:S(2)}) async-start(bf16[8,64,256]{2,1,0:T(8,128)(2,1)} %bitcast.11), calls=%async_computation.1 | async-start | bytes 524288 | tf_op jit(solution)/shard_map/all_to_all | solution.py:214
  101.4 1.1 copy.34
  102.4 6.3 %all-to-all-done.1 = bf16[8,64,256]{2,1,0:T(8,128)(2,1)S(1)} async-done(((bf16[8,64,256]{2,1,0:T(8,128)(2,1)}), bf16[8,64,256]{2,1,0:T(8,128)(2,1)S(1)}, u32[]{:S(2)}, u32[]{:S(2)}) %all-to-all-start.1) | async-done | bytes 262176 | tf_op jit(solution)/shard_map/all_to_all | solution.py:214
  108.7 0.1 reshape.179
  108.8 0.5 fusion.18
  109.3 0.2 copy.32
  109.4 0.7 copy.40
  110.1 0.2 copy.33
  110.3 0.7 copy.39
  (42 shorter events, 0.4 us)
Async XLA Ops:
  1.6 3.8 %copy-start = (bf16[512,256]{1,0:T(8,128)(2,1)}, bf16[512,256]{1,0:T(8,128)(2,1)S(1)}, u32[]{:S(2)}) copy-start(bf16[512,256]{1,0:T(8,128)(2,1)S(1)} %pad_maximum_fusion.1) | copy-start | bytes 786436
  1.6 11.0 %collective-permute-start = (bf16[4,128,256]{2,1,0:T(8,128)(2,1)S(1)}, bf16[4,128,256]{2,1,0:T(8,128)(2,1)S(1)}, u32[]{:S(2)}, u32[]{:S(2)}) collective-permute-start(bf16[4,128,256]{2,1,0:T(8,128)(2,1)S(1)} %bitcast.37), channel_id=1, source_target_pairs={{0,8},{8,16},{16,24},{24,32},{32,40},{40,48},{48,56},{56,64},{64,7... | collective-permute-start | bytes 786440 | tf_op jit(solution)/shard_map/ppermute | solution.py:20
  5.3 7.3 %copy-start.3 = (s32[256,4]{0,1:T(4,128)S(1)}, s32[256,4]{0,1:T(4,128)}, u32[]{:S(2)}) copy-start(s32[256,4]{0,1:T(4,128)} %param.10) | copy-start | bytes 12292
  5.5 29.6 %collective-permute-start.3 = (bf16[128,256]{1,0:T(8,128)(2,1)S(1)}, bf16[128,256]{1,0:T(8,128)(2,1)S(1)}, u32[]{:S(2)}, u32[]{:S(2)}) collective-permute-start(bf16[128,256]{1,0:T(8,128)(2,1)S(1)} %get-tuple-element.16), channel_id=1, source_target_pairs={{0,64},{8,72},{16,80},{24,88},{32,96},{40,104},{48,112},{56,120},{... | collective-permute-start | bytes 196616 | tf_op jit(solution)/shard_map/ppermute | solution.py:20
  13.4 11.4 %collective-permute-start.1 = (bf16[4,128,256]{2,1,0:T(8,128)(2,1)S(1)}, bf16[4,128,256]{2,1,0:T(8,128)(2,1)S(1)}, u32[]{:S(2)}, u32[]{:S(2)}) collective-permute-start(bf16[4,128,256]{2,1,0:T(8,128)(2,1)S(1)} %pad_maximum_fusion.2), channel_id=1, source_target_pairs={{0,16},{8,24},{16,32},{24,40},{32,48},{40,56},{48,64},{56,72},{64,... | collective-permute-start | bytes 786440 | tf_op jit(solution)/shard_map/ppermute | solution.py:20
  24.9 14.1 %collective-permute-start.2 = (bf16[4,128,256]{2,1,0:T(8,128)(2,1)S(1)}, bf16[4,128,256]{2,1,0:T(8,128)(2,1)S(1)}, u32[]{:S(2)}, u32[]{:S(2)}) collective-permute-start(bf16[4,128,256]{2,1,0:T(8,128)(2,1)S(1)} %pad_maximum_fusion.3), channel_id=1, source_target_pairs={{0,32},{8,40},{16,48},{24,56},{32,64},{40,72},{48,80},{56,88},{64,... | collective-permute-start | bytes 786440 | tf_op jit(solution)/shard_map/ppermute | solution.py:20
  52.7 13.9 %copy-start.2 = (bf16[4,128,256]{2,1,0:T(8,128)(2,1)S(1)}, bf16[4,128,256]{2,1,0:T(8,128)(2,1)}, u32[]{:S(2)}) copy-start(bf16[4,128,256]{2,1,0:T(8,128)(2,1)} %get-tuple-element.9) | copy-start | bytes 786436
  52.7 12.0 %collective-permute-start.4 = (bf16[4,128,256]{2,1,0:T(8,128)(2,1)}, bf16[4,128,256]{2,1,0:T(8,128)(2,1)S(1)}, u32[]{:S(2)}, u32[]{:S(2)}) collective-permute-start(bf16[4,128,256]{2,1,0:T(8,128)(2,1)} %get-tuple-element.10), channel_id=1, source_target_pairs={{32,0},{40,8},{48,16},{56,24},{64,32},{72,40},{80,48},{88,56},{96,... | collective-permute-start | bytes 786440 | tf_op jit(solution)/shard_map/ppermute | solution.py:20
  64.7 10.6 %collective-permute-start.5 = (bf16[4,128,256]{2,1,0:T(8,128)(2,1)S(1)}, bf16[4,128,256]{2,1,0:T(8,128)(2,1)S(1)}, u32[]{:S(2)}, u32[]{:S(2)}) collective-permute-start(bf16[4,128,256]{2,1,0:T(8,128)(2,1)S(1)} %pad_maximum_fusion.4), channel_id=1, source_target_pairs={{16,0},{24,8},{32,16},{40,24},{48,32},{56,40},{64,48},{72,56},{80,... | collective-permute-start | bytes 786440 | tf_op jit(solution)/shard_map/ppermute | solution.py:20
  75.3 8.2 %collective-permute-start.6 = (bf16[4,128,256]{2,1,0:T(8,128)(2,1)S(1)}, bf16[4,128,256]{2,1,0:T(8,128)(2,1)S(1)}, u32[]{:S(2)}, u32[]{:S(2)}) collective-permute-start(bf16[4,128,256]{2,1,0:T(8,128)(2,1)S(1)} %pad_maximum_fusion.5), channel_id=1, source_target_pairs={{8,0},{16,8},{24,16},{32,24},{40,32},{48,40},{56,48},{64,56},{72,6... | collective-permute-start | bytes 786440 | tf_op jit(solution)/shard_map/ppermute | solution.py:20
  77.3 20.7 %all-to-all-start = ((bf16[8,64,1024]{2,1,0:T(8,128)(2,1)}), bf16[8,64,1024]{2,1,0:T(8,128)(2,1)S(1)}, u32[]{:S(2)}, u32[]{:S(2)}) async-start(bf16[8,64,1024]{2,1,0:T(8,128)(2,1)} %bitcast.7), calls=%async_computation | async-start | bytes 2097152 | tf_op jit(solution)/shard_map/all_to_all | solution.py:209
  81.6 9.3 %collective-permute-start.7 = (bf16[128,256]{1,0:T(8,128)(2,1)S(1)}, bf16[128,256]{1,0:T(8,128)(2,1)S(1)}, u32[]{:S(2)}, u32[]{:S(2)}) collective-permute-start(bf16[128,256]{1,0:T(8,128)(2,1)S(1)} %get-tuple-element.21), channel_id=1, source_target_pairs={{64,0},{72,8},{80,16},{88,24},{96,32},{104,40},{112,48},{120,56},{... | collective-permute-start | bytes 196616 | tf_op jit(solution)/shard_map/ppermute | solution.py:20
  90.9 1.0 copy-start.1
  97.9 10.8 %all-to-all-start.1 = ((bf16[8,64,256]{2,1,0:T(8,128)(2,1)}), bf16[8,64,256]{2,1,0:T(8,128)(2,1)S(1)}, u32[]{:S(2)}, u32[]{:S(2)}) async-start(bf16[8,64,256]{2,1,0:T(8,128)(2,1)} %bitcast.11), calls=%async_computation.1 | async-start | bytes 524288 | tf_op jit(solution)/shard_map/all_to_all | solution.py:214

commit v2 on v1

--- a/solution.py
+++ b/solution.py
@@ -207,9 +207,11 @@
         chosen,
     )
     query_grad = lax.all_to_all(query_local, "head", split_axis=0, concat_axis=1, tiled=True)
-    arrived = return_tree(first, rest).astype(jnp.float32)
-    credit = (requested[None, :] == slot_ids[:, None]).astype(jnp.float32)
-    totals = home + jnp.sum(credit[:, :, None, None] * arrived[None], axis=1)
+    arrived = return_tree(first, rest)
+    totals = home
+    for d in range(REACH):
+        credit = (requested[d] == slot_ids)[:, None, None]
+        totals = totals + jnp.where(credit, arrived[d][None].astype(jnp.float32), 0.0)
     kv_grad = totals.reshape(tok_rows, 2 * kv_cols).astype(jnp.bfloat16)
     kv_all = lax.all_to_all(kv_grad, "head", split_axis=0, concat_axis=1, tiled=True)
     out_rows = tok_rows // head_count

time: 112 us -> 115 us (1.027)
  waiting for transfers between devices: 46.4 us -> 35.4 us
  starting transfers between devices: 36.9 us -> 46.4 us
  other arithmetic: 3.96 us -> 9.04 us
    all_to_all x1, starting transfers between devices: 3.41 us -> 12.7 us  [step(): lax.all_to_all(kv_grad, 'head', split_axis=0, concat_axis=1, tiled=True)]
    ppermute x8, waiting for transfers between devices: 34.9 us -> 29 us  [from_behind(): return lax.ppermute(x, axis, pairs)]
    all_to_all x1, waiting for transfers between devices: 5.2 us -> 0.01 us  [step(): lax.all_to_all(query_local, 'head', split_axis=0, concat_axis=1, tiled=True)]
    eq x0 -> x4, other arithmetic: none -> 5.06 us  [step(): credit = (requested[d] == slot_ids)[:, None, None]]
    unnamed x20 -> x13, local copies, waits for them, and re-layouts: 3.22 us -> 2.5 us
  transfers between devices with their start and end apart: 10 -> 10, of which waited for: 7 -> 6; matrix products, arithmetic and copies ran while one was open for 8% -> 12% of each run, Pallas kernels for 0% -> 0%
where the time goes in v2:
time: 115 us; the launch traced here: 114 us
  starting transfers between devices  46.4 us (40%)
  waiting for transfers between devices  35.4 us (31%)
  Pallas kernels  12.8 us (11%)
  local copies, waits for them, and re-layouts  9.77 us (8%)
  other arithmetic  9.04 us (8%)
    ppermute x8, starting transfers between devices, from_behind(): return lax.ppermute(x, axis, pairs)  29.4 us
    ppermute x8, waiting for transfers between devices, from_behind(): return lax.ppermute(x, axis, pairs)  29 us
    pallas_call x1, Pallas kernels, attention_terms(): pl.pallas_call(kernel, grid_spec=grid_spec, out_shape=[jax.ShapeDtypeStru...  12.8 us
    all_to_all x1, starting transfers between devices, step(): lax.all_to_all(kv_grad, 'head', split_axis=0, concat_axis=1, tiled=True)  12.7 us
    all_to_all x1, waiting for transfers between devices, step(): lax.all_to_all(kv_grad, 'head', split_axis=0, concat_axis=1, tiled=True)  6.45 us
    eq x4, other arithmetic, step(): credit = (requested[d] == slot_ids)[:, None, None]  5.06 us
    all_to_all x1, starting transfers between devices, step(): lax.all_to_all(query_local, 'head', split_axis=0, concat_axis=1, tiled=True)  4.34 us
    unnamed x13, local copies, waits for them, and re-layouts  2.5 us
  transfers between devices with their start and end apart: 10, of which 6 were waited for; matrix products, arithmetic and copies ran while one was open for 12% of the time, Pallas kernels for 0%

profile of v2, /device:TPU:96, one launch (start us, length us, event | category | flops | bytes accessed | tf_op | source)
XLA Modules:
  0.0 114.5 jit_solution(14377593233800764756)
XLA Ops:
  0.6 1.0 pad_maximum_fusion.1
  1.6 1.9 %collective-permute-start = (bf16[4,128,256]{2,1,0:T(8,128)(2,1)S(1)}, bf16[4,128,256]{2,1,0:T(8,128)(2,1)S(1)}, u32[]{:S(2)}, u32[]{:S(2)}) collective-permute-start(bf16[4,128,256]{2,1,0:T(8,128)(2,1)S(1)} %bitcast.78), channel_id=1, source_target_pairs={{0,8},{8,16},{16,24},{24,32},{32,40},{40,48},{48,56},{56,64},{64,7... | collective-permute-start | bytes 786440 | tf_op jit(solution)/shard_map/ppermute | solution.py:20
  3.6 0.7 copy-done.3
  4.3 0.1 copy.28
  4.4 0.1 reshape.135
  4.5 0.2 fusion.9
  4.7 0.6 gather_fusion.2
  5.3 0.1 broadcast_select_fusion
  5.5 6.4 %collective-permute-start.3 = (bf16[128,256]{1,0:T(8,128)(2,1)S(1)}, bf16[128,256]{1,0:T(8,128)(2,1)S(1)}, u32[]{:S(2)}, u32[]{:S(2)}) collective-permute-start(bf16[128,256]{1,0:T(8,128)(2,1)S(1)} %get-tuple-element.16), channel_id=1, source_target_pairs={{0,64},{8,72},{16,80},{24,88},{32,96},{40,104},{48,112},{56,120},{... | collective-permute-start | bytes 196616 | tf_op jit(solution)/shard_map/ppermute | solution.py:20
  11.9 0.6 gather_fusion
  12.7 0.6 gather_fusion.1
  13.2 0.1 broadcast_select_fusion.1
  13.4 5.1 %collective-permute-start.1 = (bf16[4,128,256]{2,1,0:T(8,128)(2,1)S(1)}, bf16[4,128,256]{2,1,0:T(8,128)(2,1)S(1)}, u32[]{:S(2)}, u32[]{:S(2)}) collective-permute-start(bf16[4,128,256]{2,1,0:T(8,128)(2,1)S(1)} %pad_maximum_fusion.2), channel_id=1, source_target_pairs={{0,16},{8,24},{16,32},{24,40},{32,48},{40,56},{48,64},{56,72},{64,... | collective-permute-start | bytes 786440 | tf_op jit(solution)/shard_map/ppermute | solution.py:20
  18.5 0.1 copy.25
  18.6 6.2 %collective-permute-done.1 = bf16[4,128,256]{2,1,0:T(8,128)(2,1)S(1)} collective-permute-done((bf16[4,128,256]{2,1,0:T(8,128)(2,1)S(1)}, bf16[4,128,256]{2,1,0:T(8,128)(2,1)S(1)}, u32[]{:S(2)}, u32[]{:S(2)}) %collective-permute-start.1) | collective-permute-done | bytes 262176 | tf_op jit(solution)/shard_map/ppermute | solution.py:20
  24.9 8.0 %collective-permute-start.2 = (bf16[4,128,256]{2,1,0:T(8,128)(2,1)S(1)}, bf16[4,128,256]{2,1,0:T(8,128)(2,1)S(1)}, u32[]{:S(2)}, u32[]{:S(2)}) collective-permute-start(bf16[4,128,256]{2,1,0:T(8,128)(2,1)S(1)} %pad_maximum_fusion.3), channel_id=1, source_target_pairs={{0,32},{8,40},{16,48},{24,56},{32,64},{40,72},{48,80},{56,88},{64,... | collective-permute-start | bytes 786440 | tf_op jit(solution)/shard_map/ppermute | solution.py:20
  32.9 0.2 and_reduce_fusion
  33.1 0.1 copy.24
  33.2 0.6 reshape.133.slot_ref
  33.8 0.6 reshape.137.use_ref
  34.4 0.1 copy.27
  34.5 0.7 reshape.138.early_ref
  35.2 3.8 %collective-permute-done.2 = bf16[4,128,256]{2,1,0:T(8,128)(2,1)S(1)} collective-permute-done((bf16[4,128,256]{2,1,0:T(8,128)(2,1)S(1)}, bf16[4,128,256]{2,1,0:T(8,128)(2,1)S(1)}, u32[]{:S(2)}, u32[]{:S(2)}) %collective-permute-start.2) | collective-permute-done | bytes 262176 | tf_op jit(solution)/shard_map/ppermute | solution.py:20
  39.0 0.9 pad_maximum_fusion.far_ref
  39.9 12.8 %shard_map.85 = (bf16[512,1024]{1,0:T(8,128)(2,1)}, f32[4,128,256]{2,1,0:T(8,128)}, bf16[4,128,256]{2,1,0:T(8,128)(2,1)}, bf16[4,128,256]{2,1,0:T(8,128)(2,1)}) custom-call(s32[16]{0:T(128)} %reshape.133.slot_ref, s32[16]{0:T(128)} %reshape.137.use_ref, s32[16]{0:T(128)} %reshape.138.early_ref, bf16[512,1024]{1,0:T(8,128)(2,1)} %q_ref.1, ...), custom_call_target="tpu_custom_call" | custom-call | tf_op jit(solution)/shard_map/pallas_call | solution.py:158
  52.7 1.9 %collective-permute-start.4 = (bf16[4,128,256]{2,1,0:T(8,128)(2,1)}, bf16[4,128,256]{2,1,0:T(8,128)(2,1)S(1)}, u32[]{:S(2)}, u32[]{:S(2)}) collective-permute-start(bf16[4,128,256]{2,1,0:T(8,128)(2,1)} %get-tuple-element.10), channel_id=1, source_target_pairs={{32,0},{40,8},{48,16},{56,24},{64,32},{72,40},{80,48},{88,56},{96,... | collective-permute-start | bytes 786440 | tf_op jit(solution)/shard_map/ppermute | solution.py:20
  54.6 0.7 fusion.28
  55.2 1.2 %iota_compare_fusion.1 = (pred[4]{0:T(512)(128)(4,1)S(1)}, pred[4]{0:T(512)(128)(4,1)S(1)}) fusion(s32[]{:T(128)} %bitcast.23, s32[]{:T(128)} %bitcast.21), kind=kLoop, calls=%fused_computation.81 | loop fusion | flops 8 | bytes 16 | tf_op jit(solution)/shard_map/eq | solution.py:213
  56.4 0.9 slice.127
  57.4 7.1 %collective-permute-done.4 = bf16[4,128,256]{2,1,0:T(8,128)(2,1)S(1)} collective-permute-done((bf16[4,128,256]{2,1,0:T(8,128)(2,1)}, bf16[4,128,256]{2,1,0:T(8,128)(2,1)S(1)}, u32[]{:S(2)}, u32[]{:S(2)}) %collective-permute-start.4) | collective-permute-done | bytes 262176 | tf_op jit(solution)/shard_map/ppermute | solution.py:20
  64.5 2.1 %collective-permute-start.5 = (bf16[4,128,256]{2,1,0:T(8,128)(2,1)S(1)}, bf16[4,128,256]{2,1,0:T(8,128)(2,1)S(1)}, u32[]{:S(2)}, u32[]{:S(2)}) collective-permute-start(bf16[4,128,256]{2,1,0:T(8,128)(2,1)S(1)} %pad_maximum_fusion.4), channel_id=1, source_target_pairs={{16,0},{24,8},{32,16},{40,24},{48,32},{56,40},{64,48},{72,56},{80,... | collective-permute-start | bytes 786440 | tf_op jit(solution)/shard_map/ppermute | solution.py:20
  66.6 4.3 %all-to-all-start = ((bf16[8,64,1024]{2,1,0:T(8,128)(2,1)}), bf16[8,64,1024]{2,1,0:T(8,128)(2,1)S(1)}, u32[]{:S(2)}, u32[]{:S(2)}) async-start(bf16[8,64,1024]{2,1,0:T(8,128)(2,1)} %bitcast.7), calls=%async_computation | async-start | bytes 2097152 | tf_op jit(solution)/shard_map/all_to_all | solution.py:209
  71.0 5.5 %collective-permute-done.5 = bf16[4,128,256]{2,1,0:T(8,128)(2,1)S(1)} collective-permute-done((bf16[4,128,256]{2,1,0:T(8,128)(2,1)S(1)}, bf16[4,128,256]{2,1,0:T(8,128)(2,1)S(1)}, u32[]{:S(2)}, u32[]{:S(2)}) %collective-permute-start.5) | collective-permute-done | bytes 262176 | tf_op jit(solution)/shard_map/ppermute | solution.py:20
  76.6 2.1 %collective-permute-start.6 = (bf16[4,128,256]{2,1,0:T(8,128)(2,1)S(1)}, bf16[4,128,256]{2,1,0:T(8,128)(2,1)S(1)}, u32[]{:S(2)}, u32[]{:S(2)}) collective-permute-start(bf16[4,128,256]{2,1,0:T(8,128)(2,1)S(1)} %pad_maximum_fusion.5), channel_id=1, source_target_pairs={{8,0},{16,8},{24,16},{32,24},{40,32},{48,40},{56,48},{64,56},{72,6... | collective-permute-start | bytes 786440 | tf_op jit(solution)/shard_map/ppermute | solution.py:20
  78.7 1.3 %iota_compare_fusion.3 = (pred[4]{0:T(512)(128)(4,1)S(1)}, pred[4]{0:T(512)(128)(4,1)S(1)}) fusion(s32[]{:T(128)} %bitcast.19, s32[]{:T(128)} %bitcast.17), kind=kLoop, calls=%fused_computation.83 | loop fusion | flops 8 | bytes 16 | tf_op jit(solution)/shard_map/eq | solution.py:213
  79.9 1.3 %iota_compare_fusion.5 = (pred[4]{0:T(512)(128)(4,1)S(1)}, pred[4]{0:T(512)(128)(4,1)S(1)}) fusion(s32[]{:T(128)} %bitcast.15, s32[]{:T(128)} %bitcast.13), kind=kLoop, calls=%fused_computation.85 | loop fusion | flops 8 | bytes 16 | tf_op jit(solution)/shard_map/eq | solution.py:213
  81.2 1.9 %collective-permute-start.7 = (bf16[128,256]{1,0:T(8,128)(2,1)S(1)}, bf16[128,256]{1,0:T(8,128)(2,1)S(1)}, u32[]{:S(2)}, u32[]{:S(2)}) collective-permute-start(bf16[128,256]{1,0:T(8,128)(2,1)S(1)} %get-tuple-element.32), channel_id=1, source_target_pairs={{64,0},{72,8},{80,16},{88,24},{96,32},{104,40},{112,48},{120,56},{... | collective-permute-start | bytes 196616 | tf_op jit(solution)/shard_map/ppermute | solution.py:20
  83.1 1.3 %iota_compare_fusion.7 = (pred[4]{0:T(512)(128)(4,1)S(1)}, pred[4]{0:T(512)(128)(4,1)S(1)}) fusion(s32[]{:T(128)} %bitcast.11, s32[]{:T(128)} %bitcast.9), kind=kLoop, calls=%fused_computation.87 | loop fusion | flops 8 | bytes 16 | tf_op jit(solution)/shard_map/eq | solution.py:213
  84.5 6.3 %collective-permute-done.7 = bf16[128,256]{1,0:T(8,128)(2,1)S(1)} collective-permute-done((bf16[128,256]{1,0:T(8,128)(2,1)S(1)}, bf16[128,256]{1,0:T(8,128)(2,1)S(1)}, u32[]{:S(2)}, u32[]{:S(2)}) %collective-permute-start.7) | collective-permute-done | bytes 65568 | tf_op jit(solution)/shard_map/ppermute | solution.py:20
  90.9 1.1 add_convert_fusion
  92.0 12.7 %all-to-all-start.1 = ((bf16[8,64,256]{2,1,0:T(8,128)(2,1)}), bf16[8,64,256]{2,1,0:T(8,128)(2,1)S(1)}, u32[]{:S(2)}, u32[]{:S(2)}) async-start(bf16[8,64,256]{2,1,0:T(8,128)(2,1)} %bitcast.25), calls=%async_computation.1 | async-start | bytes 524288 | tf_op jit(solution)/shard_map/all_to_all | solution.py:216
  104.7 1.1 copy.34
  105.8 6.4 %all-to-all-done.1 = bf16[8,64,256]{2,1,0:T(8,128)(2,1)S(1)} async-done(((bf16[8,64,256]{2,1,0:T(8,128)(2,1)}), bf16[8,64,256]{2,1,0:T(8,128)(2,1)S(1)}, u32[]{:S(2)}, u32[]{:S(2)}) %all-to-all-start.1) | async-done | bytes 262176 | tf_op jit(solution)/shard_map/all_to_all | solution.py:216
  112.3 0.5 fusion.24
  112.8 0.2 copy.33
  112.9 0.7 copy.39
  113.6 0.2 copy.32
  113.8 0.7 copy.40
  (39 shorter events, 0.6 us)
Async XLA Ops:
  1.6 3.7 %copy-start = (bf16[512,256]{1,0:T(8,128)(2,1)}, bf16[512,256]{1,0:T(8,128)(2,1)S(1)}, u32[]{:S(2)}) copy-start(bf16[512,256]{1,0:T(8,128)(2,1)S(1)} %pad_maximum_fusion.1) | copy-start | bytes 786436
  1.6 11.0 %collective-permute-start = (bf16[4,128,256]{2,1,0:T(8,128)(2,1)S(1)}, bf16[4,128,256]{2,1,0:T(8,128)(2,1)S(1)}, u32[]{:S(2)}, u32[]{:S(2)}) collective-permute-start(bf16[4,128,256]{2,1,0:T(8,128)(2,1)S(1)} %bitcast.78), channel_id=1, source_target_pairs={{0,8},{8,16},{16,24},{24,32},{32,40},{40,48},{48,56},{56,64},{64,7... | collective-permute-start | bytes 786440 | tf_op jit(solution)/shard_map/ppermute | solution.py:20
  3.6 0.7 copy-start.3
  5.5 29.7 %collective-permute-start.3 = (bf16[128,256]{1,0:T(8,128)(2,1)S(1)}, bf16[128,256]{1,0:T(8,128)(2,1)S(1)}, u32[]{:S(2)}, u32[]{:S(2)}) collective-permute-start(bf16[128,256]{1,0:T(8,128)(2,1)S(1)} %get-tuple-element.16), channel_id=1, source_target_pairs={{0,64},{8,72},{16,80},{24,88},{32,96},{40,104},{48,112},{56,120},{... | collective-permute-start | bytes 196616 | tf_op jit(solution)/shard_map/ppermute | solution.py:20
  13.4 11.4 %collective-permute-start.1 = (bf16[4,128,256]{2,1,0:T(8,128)(2,1)S(1)}, bf16[4,128,256]{2,1,0:T(8,128)(2,1)S(1)}, u32[]{:S(2)}, u32[]{:S(2)}) collective-permute-start(bf16[4,128,256]{2,1,0:T(8,128)(2,1)S(1)} %pad_maximum_fusion.2), channel_id=1, source_target_pairs={{0,16},{8,24},{16,32},{24,40},{32,48},{40,56},{48,64},{56,72},{64,... | collective-permute-start | bytes 786440 | tf_op jit(solution)/shard_map/ppermute | solution.py:20
  24.9 14.1 %collective-permute-start.2 = (bf16[4,128,256]{2,1,0:T(8,128)(2,1)S(1)}, bf16[4,128,256]{2,1,0:T(8,128)(2,1)S(1)}, u32[]{:S(2)}, u32[]{:S(2)}) collective-permute-start(bf16[4,128,256]{2,1,0:T(8,128)(2,1)S(1)} %pad_maximum_fusion.3), channel_id=1, source_target_pairs={{0,32},{8,40},{16,48},{24,56},{32,64},{40,72},{48,80},{56,88},{64,... | collective-permute-start | bytes 786440 | tf_op jit(solution)/shard_map/ppermute | solution.py:20
  52.7 11.8 %collective-permute-start.4 = (bf16[4,128,256]{2,1,0:T(8,128)(2,1)}, bf16[4,128,256]{2,1,0:T(8,128)(2,1)S(1)}, u32[]{:S(2)}, u32[]{:S(2)}) collective-permute-start(bf16[4,128,256]{2,1,0:T(8,128)(2,1)} %get-tuple-element.10), channel_id=1, source_target_pairs={{32,0},{40,8},{48,16},{56,24},{64,32},{72,40},{80,48},{88,56},{96,... | collective-permute-start | bytes 786440 | tf_op jit(solution)/shard_map/ppermute | solution.py:20
  64.5 2.1 %copy-start.2 = (bf16[4,128,256]{2,1,0:T(8,128)(2,1)S(1)}, bf16[4,128,256]{2,1,0:T(8,128)(2,1)}, u32[]{:S(2)}) copy-start(bf16[4,128,256]{2,1,0:T(8,128)(2,1)} %get-tuple-element.9) | copy-start | bytes 786436
  64.5 12.0 %collective-permute-start.5 = (bf16[4,128,256]{2,1,0:T(8,128)(2,1)S(1)}, bf16[4,128,256]{2,1,0:T(8,128)(2,1)S(1)}, u32[]{:S(2)}, u32[]{:S(2)}) collective-permute-start(bf16[4,128,256]{2,1,0:T(8,128)(2,1)S(1)} %pad_maximum_fusion.4), channel_id=1, source_target_pairs={{16,0},{24,8},{32,16},{40,24},{48,32},{56,40},{64,48},{72,56},{80,... | collective-permute-start | bytes 786440 | tf_op jit(solution)/shard_map/ppermute | solution.py:20
  66.6 25.4 %all-to-all-start = ((bf16[8,64,1024]{2,1,0:T(8,128)(2,1)}), bf16[8,64,1024]{2,1,0:T(8,128)(2,1)S(1)}, u32[]{:S(2)}, u32[]{:S(2)}) async-start(bf16[8,64,1024]{2,1,0:T(8,128)(2,1)} %bitcast.7), calls=%async_computation | async-start | bytes 2097152 | tf_op jit(solution)/shard_map/all_to_all | solution.py:209
  76.6 14.3 %copy-start.1 = (f32[4,128,256]{2,1,0:T(8,128)S(1)}, f32[4,128,256]{2,1,0:T(8,128)}, u32[]{:S(2)}) copy-start(f32[4,128,256]{2,1,0:T(8,128)} %get-tuple-element.8) | copy-start | bytes 1572868
  76.6 14.2 %collective-permute-start.6 = (bf16[4,128,256]{2,1,0:T(8,128)(2,1)S(1)}, bf16[4,128,256]{2,1,0:T(8,128)(2,1)S(1)}, u32[]{:S(2)}, u32[]{:S(2)}) collective-permute-start(bf16[4,128,256]{2,1,0:T(8,128)(2,1)S(1)} %pad_maximum_fusion.5), channel_id=1, source_target_pairs={{8,0},{16,8},{24,16},{32,24},{40,32},{48,40},{56,48},{64,56},{72,6... | collective-permute-start | bytes 786440 | tf_op jit(solution)/shard_map/ppermute | solution.py:20
  81.2 9.6 %collective-permute-start.7 = (bf16[128,256]{1,0:T(8,128)(2,1)S(1)}, bf16[128,256]{1,0:T(8,128)(2,1)S(1)}, u32[]{:S(2)}, u32[]{:S(2)}) collective-permute-start(bf16[128,256]{1,0:T(8,128)(2,1)S(1)} %get-tuple-element.32), channel_id=1, source_target_pairs={{64,0},{72,8},{80,16},{88,24},{96,32},{104,40},{112,48},{120,56},{... | collective-permute-start | bytes 196616 | tf_op jit(solution)/shard_map/ppermute | solution.py:20
  92.0 20.2 %all-to-all-start.1 = ((bf16[8,64,256]{2,1,0:T(8,128)(2,1)}), bf16[8,64,256]{2,1,0:T(8,128)(2,1)S(1)}, u32[]{:S(2)}, u32[]{:S(2)}) async-start(bf16[8,64,256]{2,1,0:T(8,128)(2,1)} %bitcast.25), calls=%async_computation.1 | async-start | bytes 524288 | tf_op jit(solution)/shard_map/all_to_all | solution.py:216
